TPU v7x, 32 devices: a whole 2x2x4 slice. The times are simulated.
32 devices in a mesh: group: 2 (over core), gx: 4 (over y, x), gy: 4 (over z).
Axes of the slice: x: 2, y: 2, z: 4, core: 2. Of those that a mesh axis runs over, the one named last changes fastest.
Arguments:
- gradient_windows: bfloat16 [2, 4, 4, 256, 4, 2, 128], P('group', 'gx', 'gy'), may hold values from -6 to 6
- illumination_windows: bfloat16 [2, 4, 4, 256, 4, 2, 128], P('group', 'gx', 'gy'), may hold values from 0.25 to 8
- window_owners: int32 [2, 4, 4, 256], P('group', 'gx', 'gy'), may hold values from 0 to 15, as said below
- window_patches: int32 [2, 4, 4, 256], P('group', 'gx', 'gy'), may hold values from 0 to 7
- velocity: float32 [4, 64, 512], P(None, 'gx', 'gy'), may hold values from 1.5 to 4.5
Outputs:
- updated_model: float32 [4, 64, 512], P(None, 'gx', 'gy')
- returned_windows: bfloat16 [2, 4, 4, 256, 4, 2, 128], P('group', 'gx', 'gy')
Inputs may be any that keep to these rules, and one draw needn't show every extreme that they name: `window_owners`: the window patches of one device name any tile at most 20 times; one tile is named exactly 20 times by the window patches of every device.
All inputs are finite; a program needn't handle non-finite values.
Results may differ from a plain program's by a relative error of at most 0.001.
Values may be sent and summed in bfloat16 or wider, within the bound.
No kernel may reach another device: no remote copies, remote signals or barrier semaphores. Data moves between devices by JAX's collectives and lax.ppermute only.
A program may use at most 64 MiB of HBM per device.

v0:
```python
import jax
import jax.numpy as jnp
from jax import lax
from jax.sharding import PartitionSpec as P

SWEEPS = 4
damping = 10.0
smooth_rate = 0.12
step_length = 24.0


def with_halo(cells, sides, width):
    for axis, dim in sides:
        count = lax.axis_size(axis)
        ends = count - 1
        head = lax.slice_in_dim(cells, 0, width, axis=dim)
        tail = lax.slice_in_dim(cells, cells.shape[dim] - width, cells.shape[dim], axis=dim)
        cells = jnp.concatenate(
            [
                lax.ppermute(tail, axis, [(i, (i + 1) % count) for i in range(ends)]),
                cells,
                lax.ppermute(head, axis, [((i + 1) % count, i) for i in range(ends)]),
            ],
            axis=dim,
        )
    return cells


def deliver(send_grad, send_illum, send_patch, size_x, size_y, capacity):
    sectioned_grad = send_grad.reshape((size_x, size_y, capacity) + send_grad.shape[1:])
    sectioned_illum = send_illum.reshape((size_x, size_y, capacity) + send_illum.shape[1:])
    sectioned_patch = send_patch.reshape(size_x, size_y, capacity)
    got_grad, got_illum, got_patch = (
        lax.all_to_all(
            lax.all_to_all(sectioned_grad, "gx", split_axis=0, concat_axis=0, tiled=True),
            "gy",
            split_axis=1,
            concat_axis=1,
            tiled=True,
        ),
        lax.all_to_all(
            lax.all_to_all(sectioned_illum, "gx", split_axis=0, concat_axis=0, tiled=True),
            "gy",
            split_axis=1,
            concat_axis=1,
            tiled=True,
        ),
        lax.all_to_all(
            lax.all_to_all(sectioned_patch, "gx", split_axis=0, concat_axis=0, tiled=True),
            "gy",
            split_axis=1,
            concat_axis=1,
            tiled=True,
        ),
    )
    return (
        got_grad.reshape(send_grad.shape),
        got_illum.reshape(send_illum.shape),
        got_patch.reshape(send_patch.shape),
    )


def send_back(back_rows, size_x, size_y, capacity):
    sectioned_back = back_rows.reshape((size_x, size_y, capacity) + back_rows.shape[1:])
    arrived = lax.all_to_all(
        lax.all_to_all(sectioned_back, "gx", split_axis=0, concat_axis=0, tiled=True),
        "gy",
        split_axis=1,
        concat_axis=1,
        tiled=True,
    )
    return arrived.reshape(back_rows.shape)


def smooth_whole(field_now):
    for sweep_index in range(SWEEPS):
        padded = with_halo(field_now, (("gx", 1), ("gy", 2)), 1)
        depth_pad = jnp.pad(field_now, ((1, 1), (0, 0), (0, 0)))
        beside = (
            padded[:, 2:, 1:-1]
            + padded[:, :-2, 1:-1]
            + (padded[:, 1:-1, 2:] + padded[:, 1:-1, :-2])
            + (depth_pad[2:] + depth_pad[:-2])
        )
        field_now = field_now + smooth_rate * (beside - 6.0 * field_now)
    return field_now


def local(gradient_windows, illumination_windows, window_owners, window_patches, velocity):
    size_x = lax.axis_size("gx")
    size_y = lax.axis_size("gy")
    holder_count = size_x * size_y
    slot_grad = gradient_windows[0, 0, 0]
    slot_illum = illumination_windows[0, 0, 0]
    owners = window_owners[0, 0, 0]
    patches = window_patches[0, 0, 0]
    slot_count, levels, patch_rows, patch_cols = slot_grad.shape
    patch_count = velocity.shape[1] // patch_rows
    mean_load = slot_count // holder_count
    capacity = mean_load + max(1, slot_count // (4 * holder_count))
    rows_total = holder_count * capacity
    cell_count = levels * patch_rows * patch_cols
    member = (owners[:, None] == jnp.arange(holder_count, dtype=jnp.int32)[None, :]).astype(
        jnp.int32
    )
    slot_rank = jnp.sum(jnp.cumsum(member, axis=0) * member, axis=1) - 1
    position = owners * capacity + slot_rank
    send_grad = (
        jnp.zeros((rows_total, levels, patch_rows, patch_cols), jnp.bfloat16)
        .at[position]
        .set(slot_grad)
    )
    send_illum = (
        jnp.zeros((rows_total, levels, patch_rows, patch_cols), jnp.bfloat16)
        .at[position]
        .set(slot_illum)
    )
    send_patch = jnp.full((rows_total,), -1, jnp.int32).at[position].set(patches)
    got_grad, got_illum, got_patch = deliver(
        send_grad, send_illum, send_patch, size_x, size_y, capacity
    )
    onehot = (got_patch[None, :] == jnp.arange(patch_count, dtype=jnp.int32)[:, None]).astype(
        jnp.bfloat16
    )
    grad_sum = jnp.dot(
        onehot, got_grad.reshape(rows_total, cell_count), preferred_element_type=jnp.float32
    )
    illum_sum = jnp.dot(
        onehot, got_illum.reshape(rows_total, cell_count), preferred_element_type=jnp.float32
    )

    def to_tile(patch_sums):
        return (
            patch_sums.reshape(patch_count, levels, patch_rows, patch_cols)
            .transpose(1, 0, 2, 3)
            .reshape(levels, patch_count * patch_rows, patch_cols)
        )

    grad_total, illum_total = lax.psum((to_tile(grad_sum), to_tile(illum_sum)), "group")
    smoothed = smooth_whole(grad_total / (illum_total + damping))
    updated_model = velocity - step_length * smoothed
    patch_table = (
        updated_model.reshape(levels, patch_count, patch_rows, patch_cols)
        .transpose(1, 0, 2, 3)
        .reshape(patch_count, cell_count)
        .astype(jnp.bfloat16)
    )
    back_rows = jnp.dot(onehot.T, patch_table, preferred_element_type=jnp.float32).astype(
        jnp.bfloat16
    )
    back_rows = back_rows.reshape(rows_total, levels, patch_rows, patch_cols)
    arrived = send_back(back_rows, size_x, size_y, capacity)
    returned = jnp.take(arrived, position, axis=0)
    returned_windows = returned.reshape((1, 1, 1) + returned.shape)
    return (updated_model, returned_windows)


def solution(mesh):
    return jax.shard_map(
        local,
        mesh=mesh,
        in_specs=(
            P("group", "gx", "gy", None, None, None, None),
            P("group", "gx", "gy", None, None, None, None),
            P("group", "gx", "gy", None),
            P("group", "gx", "gy", None),
            P(None, "gx", "gy"),
        ),
        out_specs=(P(None, "gx", "gy"), P("group", "gx", "gy", None, None, None, None)),
        check_vma=False,
    )
```

profile of v0, /device:TPU:0, one launch (start us, length us, event | category | flops | bytes accessed | tf_op | source)
XLA Modules:
  0.0 227.5 jit_solution(14534622303721739606)
XLA Ops:
  7.2 0.7 fusion.38
  7.8 0.6 reduce-window.6
  8.6 0.8 fusion.37
  9.4 0.7 compare_select_fusion
  10.1 1.6 scatter_custom_fusion
  11.8 9.7 %all_to_all.40 = s32[4,4,20]{2,1,0:T(4,128)S(1)} all-to-all(s32[4,4,20]{2,1,0:T(4,128)S(1)} %reshape.97), channel_id=1, replica_groups=mesh['group'=2,'gx'=4,'gy'=4] {'gx'}, dimensions={0} | all-to-all | bytes 2560 | tf_op jit(solution)/shard_map/all_to_all | solution.py:49
  21.4 0.6 copy.49
  22.0 4.9 %all-to-all-start.1 = ((s32[4,4,20]{2,0,1:T(4,128)}), s32[4,4,20]{2,0,1:T(4,128)S(1)}, u32[]{:S(2)}, u32[]{:S(2)}) async-start(s32[4,4,20]{2,0,1:T(4,128)} %copy.49), calls=%async_computation.1 | async-start | bytes 16384 | tf_op jit(solution)/shard_map/all_to_all | solution.py:48
  26.9 1.2 copy.57
  28.3 7.1 %scatter_fusion.1 = bf16[320,4,2,128]{3,1,2,0:T(4,128)(2,1)S(1)} fusion(bf16[320,4,2,128]{3,1,2,0:T(4,128)(2,1)S(1)} %broadcast.109.clone.1, s32[256]{0:T(256)S(1)} %bitcast.69, bf16[256,4,2,128]{3,1,2,0:T(4,128)(2,1)S(1)} %copy.57), kind=kCustom, calls=%fused_computation.3 | custom fusion | bytes 1573888 | tf_op jit(solution)/shard_map/scatter | solution.py:116
  35.4 1.5 copy.58
  36.9 3.6 %all-to-all-start.4 = ((bf16[4,4,20,4,2,128]{5,4,3,2,1,0:T(2,128)(2,1)}), bf16[4,4,20,4,2,128]{5,4,3,2,1,0:T(2,128)(2,1)S(1)}, u32[]{:S(2)}, u32[]{:S(2)}) async-start(bf16[4,4,20,4,2,128]{5,4,3,2,1,0:T(2,128)(2,1)} %copy.58), calls=%async_computation.4 | async-start | bytes 1310720 | tf_op jit(solution)/shard_map/all_to_all | solution.py:42
  40.9 7.1 %scatter_fusion = bf16[320,4,2,128]{3,1,2,0:T(4,128)(2,1)S(1)} fusion(bf16[320,4,2,128]{3,1,2,0:T(4,128)(2,1)S(1)} %broadcast.109.clone, s32[256]{0:T(256)S(1)} %bitcast.70, bf16[256,4,2,128]{3,1,2,0:T(4,128)(2,1)S(1)} %copy.51), kind=kCustom, calls=%fused_computation.2 | custom fusion | bytes 1573888 | tf_op jit(solution)/shard_map/scatter | solution.py:111
  48.0 1.5 copy.52
  49.5 4.1 %all-to-all-start.2 = ((bf16[4,4,20,4,2,128]{5,4,3,2,1,0:T(2,128)(2,1)}), bf16[4,4,20,4,2,128]{5,4,3,2,1,0:T(2,128)(2,1)S(1)}, u32[]{:S(2)}, u32[]{:S(2)}) async-start(bf16[4,4,20,4,2,128]{5,4,3,2,1,0:T(2,128)(2,1)} %copy.52), calls=%async_computation.2 | async-start | bytes 1310720 | tf_op jit(solution)/shard_map/all_to_all | solution.py:35
  53.7 1.3 copy.59
  55.0 6.1 %all-to-all-done.2 = bf16[4,4,20,4,2,128]{5,4,3,2,1,0:T(2,128)(2,1)S(1)} async-done(((bf16[4,4,20,4,2,128]{5,4,3,2,1,0:T(2,128)(2,1)}), bf16[4,4,20,4,2,128]{5,4,3,2,1,0:T(2,128)(2,1)S(1)}, u32[]{:S(2)}, u32[]{:S(2)}) %all-to-all-start.2) | async-done | bytes 655392 | tf_op jit(solution)/shard_map/all_to_all | solution.py:35
  61.1 4.9 %all-to-all-start.5 = ((bf16[4,4,20,4,2,128]{5,4,3,2,0,1:T(2,128)(2,1)}), bf16[4,4,20,4,2,128]{5,4,3,2,0,1:T(2,128)(2,1)S(1)}, u32[]{:S(2)}, u32[]{:S(2)}) async-start(bf16[4,4,20,4,2,128]{5,4,3,2,0,1:T(2,128)(2,1)} %copy.59), calls=%async_computation.5 | async-start | bytes 1310720 | tf_op jit(solution)/shard_map/all_to_all | solution.py:41
  66.1 1.3 copy.53
  67.4 12.3 %all-to-all-done.5 = bf16[4,4,20,4,2,128]{5,4,3,2,0,1:T(2,128)(2,1)S(1)} async-done(((bf16[4,4,20,4,2,128]{5,4,3,2,0,1:T(2,128)(2,1)}), bf16[4,4,20,4,2,128]{5,4,3,2,0,1:T(2,128)(2,1)S(1)}, u32[]{:S(2)}, u32[]{:S(2)}) %all-to-all-start.5) | async-done | bytes 655392 | tf_op jit(solution)/shard_map/all_to_all | solution.py:41
  79.7 3.5 %all-to-all-start.3 = ((bf16[4,4,20,4,2,128]{5,4,3,2,0,1:T(2,128)(2,1)}), bf16[4,4,20,4,2,128]{5,4,3,2,0,1:T(2,128)(2,1)S(1)}, u32[]{:S(2)}, u32[]{:S(2)}) async-start(bf16[4,4,20,4,2,128]{5,4,3,2,0,1:T(2,128)(2,1)} %copy.53), calls=%async_computation.3 | async-start | bytes 1310720 | tf_op jit(solution)/shard_map/all_to_all | solution.py:34
  83.3 0.5 copy.60
  83.8 0.5 reshape_reshape.10
  84.3 0.5 dot_general.21
  84.9 0.6 copy.62
  85.6 12.3 %all-to-all-done.3 = bf16[4,4,20,4,2,128]{5,4,3,2,0,1:T(2,128)(2,1)S(1)} async-done(((bf16[4,4,20,4,2,128]{5,4,3,2,0,1:T(2,128)(2,1)}), bf16[4,4,20,4,2,128]{5,4,3,2,0,1:T(2,128)(2,1)S(1)}, u32[]{:S(2)}, u32[]{:S(2)}) %all-to-all-start.3) | async-done | bytes 655392 | tf_op jit(solution)/shard_map/all_to_all | solution.py:34
  97.9 0.5 copy.54
  98.3 0.5 reshape_reshape.9
  98.8 0.5 dot_general.18
  99.5 0.6 copy.56
  100.1 16.3 %all-reduce.7.cloned.1.call-done = (f32[4,16,128]{2,1,0:T(8,128)}, f32[4,16,128]{2,1,0:T(8,128)}) async-done(((f32[4,16,128]{2,1,0:T(8,128)}, f32[4,16,128]{2,1,0:T(8,128)}), (f32[4,16,128]{2,1,0:T(8,128)}, f32[4,16,128]{2,1,0:T(8,128)})) %all-reduce.7.cloned.1.call-update) | async-done | bytes 65552 | tf_op jit(solution)/shard_map/psum | solution.py:139
  116.5 0.8 add_divide_fusion
  117.3 1.3 collective-permute-start
  118.6 4.5 %collective-permute-start.1 = (f32[4,1,128]{2,1,0:T(1,128)S(1)}, f32[4,1,128]{2,1,0:T(1,128)S(1)}, u32[]{:S(2)}, u32[]{:S(2)}) collective-permute-start(f32[4,1,128]{2,1,0:T(1,128)S(1)} %get-tuple-element.20), channel_id=1, source_target_pairs={{0,4},{4,8},{8,12},{1,5},{5,9},{9,13},{2,6},{6,10},{10,14},{3,7},{... | collective-permute-start | bytes 6152 | tf_op jit(solution)/shard_map/ppermute | solution.py:20
  123.1 1.3 collective-permute-done.1
  124.5 1.3 collective-permute-start.2
  125.8 4.5 %collective-permute-start.3 = (f32[4,18,1]{2,1,0:T(8,128)S(1)}, f32[4,18,1]{2,1,0:T(8,128)S(1)}, u32[]{:S(2)}, u32[]{:S(2)}) collective-permute-start(f32[4,18,1]{2,1,0:T(8,128)S(1)} %get-tuple-element.13), channel_id=1, source_target_pairs={{0,1},{1,2},{2,3},{4,5},{5,6},{6,7},{8,9},{9,10},{10,11},{12,13},{... | collective-permute-start | bytes 872 | tf_op jit(solution)/shard_map/ppermute | solution.py:20
  130.5 1.6 collective-permute-done.3
  132.2 1.3 collective-permute-start.4
  133.5 5.2 %collective-permute-start.5 = (f32[4,1,128]{2,1,0:T(1,128)S(1)}, f32[4,1,128]{2,1,0:T(1,128)S(1)}, u32[]{:S(2)}, u32[]{:S(2)}) collective-permute-start(f32[4,1,128]{2,1,0:T(1,128)S(1)} %get-tuple-element.18), channel_id=1, source_target_pairs={{0,4},{4,8},{8,12},{1,5},{5,9},{9,13},{2,6},{6,10},{10,14},{3,7},{... | collective-permute-start | bytes 6152 | tf_op jit(solution)/shard_map/ppermute | solution.py:20
  138.7 1.3 collective-permute-done.5
  140.1 1.3 collective-permute-start.6
  141.4 4.9 %collective-permute-start.7 = (f32[4,18,1]{2,1,0:T(8,128)S(1)}, f32[4,18,1]{2,1,0:T(8,128)S(1)}, u32[]{:S(2)}, u32[]{:S(2)}) collective-permute-start(f32[4,18,1]{2,1,0:T(8,128)S(1)} %get-tuple-element.11), channel_id=1, source_target_pairs={{0,1},{1,2},{2,3},{4,5},{5,6},{6,7},{8,9},{9,10},{10,11},{12,13},{... | collective-permute-start | bytes 872 | tf_op jit(solution)/shard_map/ppermute | solution.py:20
  146.4 1.6 collective-permute-done.7
  148.1 1.3 collective-permute-start.8
  149.4 5.7 %collective-permute-start.9 = (f32[4,1,128]{2,1,0:T(1,128)S(1)}, f32[4,1,128]{2,1,0:T(1,128)S(1)}, u32[]{:S(2)}, u32[]{:S(2)}) collective-permute-start(f32[4,1,128]{2,1,0:T(1,128)S(1)} %get-tuple-element.16), channel_id=1, source_target_pairs={{0,4},{4,8},{8,12},{1,5},{5,9},{9,13},{2,6},{6,10},{10,14},{3,7},{... | collective-permute-start | bytes 6152 | tf_op jit(solution)/shard_map/ppermute | solution.py:20
  155.1 1.3 collective-permute-done.9
  156.5 1.3 collective-permute-start.10
  157.8 4.9 %collective-permute-start.11 = (f32[4,18,1]{2,1,0:T(8,128)S(1)}, f32[4,18,1]{2,1,0:T(8,128)S(1)}, u32[]{:S(2)}, u32[]{:S(2)}) collective-permute-start(f32[4,18,1]{2,1,0:T(8,128)S(1)} %get-tuple-element.9), channel_id=1, source_target_pairs={{0,1},{1,2},{2,3},{4,5},{5,6},{6,7},{8,9},{9,10},{10,11},{12,13},{... | collective-permute-start | bytes 872 | tf_op jit(solution)/shard_map/ppermute | solution.py:20
  162.8 1.6 collective-permute-done.11
  164.6 1.3 collective-permute-start.12
  165.9 5.7 %collective-permute-start.13 = (f32[4,1,128]{2,1,0:T(1,128)S(1)}, f32[4,1,128]{2,1,0:T(1,128)S(1)}, u32[]{:S(2)}, u32[]{:S(2)}) collective-permute-start(f32[4,1,128]{2,1,0:T(1,128)S(1)} %get-tuple-element.14), channel_id=1, source_target_pairs={{0,4},{4,8},{8,12},{1,5},{5,9},{9,13},{2,6},{6,10},{10,14},{3,7},{... | collective-permute-start | bytes 6152 | tf_op jit(solution)/shard_map/ppermute | solution.py:20
  171.6 1.3 collective-permute-done.13
  172.9 1.3 collective-permute-start.14
  174.2 4.9 %collective-permute-start.15 = (f32[4,18,1]{2,1,0:T(8,128)S(1)}, f32[4,18,1]{2,1,0:T(8,128)S(1)}, u32[]{:S(2)}, u32[]{:S(2)}) collective-permute-start(f32[4,18,1]{2,1,0:T(8,128)S(1)} %get-tuple-element.7), channel_id=1, source_target_pairs={{0,1},{1,2},{2,3},{4,5},{5,6},{6,7},{8,9},{9,10},{10,11},{12,13},{... | collective-permute-start | bytes 872 | tf_op jit(solution)/shard_map/ppermute | solution.py:20
  179.3 1.6 collective-permute-done.15
  180.9 0.7 fusion.47
  182.0 0.5 reshape_reshape.11
  182.4 14.3 %all_to_all.41 = bf16[4,4,20,4,2,128]{5,4,3,2,1,0:T(2,128)(2,1)S(1)} all-to-all(bf16[4,4,20,4,2,128]{5,4,3,2,1,0:T(2,128)(2,1)S(1)} %reshape_reshape.11), channel_id=1, replica_groups=mesh['group'=2,'gx'=4,'gy'=4] {'gx'}, dimensions={0} | all-to-all | bytes 1310720 | tf_op jit(solution)/shard_map/all_to_all | solution.py:66
  196.8 1.3 copy.64
  198.1 6.8 %all-to-all-start.7 = ((bf16[4,4,20,4,2,128]{5,4,3,2,0,1:T(2,128)(2,1)}), bf16[4,4,20,4,2,128]{5,4,3,2,0,1:T(2,128)(2,1)S(1)}, u32[]{:S(2)}, u32[]{:S(2)}) async-start(bf16[4,4,20,4,2,128]{5,4,3,2,0,1:T(2,128)(2,1)} %copy.64), calls=%async_computation.7 | async-start | bytes 1310720 | tf_op jit(solution)/shard_map/all_to_all | solution.py:65
  205.0 11.7 %all-to-all-done.7 = bf16[4,4,20,4,2,128]{5,4,3,2,0,1:T(2,128)(2,1)S(1)} async-done(((bf16[4,4,20,4,2,128]{5,4,3,2,0,1:T(2,128)(2,1)}), bf16[4,4,20,4,2,128]{5,4,3,2,0,1:T(2,128)(2,1)S(1)}, u32[]{:S(2)}, u32[]{:S(2)}) %all-to-all-start.7) | async-done | bytes 655392 | tf_op jit(solution)/shard_map/all_to_all | solution.py:65
  217.1 1.7 gather_fusion
  218.9 1.7 broadcast_select_fusion
  (50 shorter events, 3.5 us)
Async XLA Ops:
  22.0 14.9 %all-to-all-start.1 = ((s32[4,4,20]{2,0,1:T(4,128)}), s32[4,4,20]{2,0,1:T(4,128)S(1)}, u32[]{:S(2)}, u32[]{:S(2)}) async-start(s32[4,4,20]{2,0,1:T(4,128)} %copy.49), calls=%async_computation.1 | async-start | bytes 16384 | tf_op jit(solution)/shard_map/all_to_all | solution.py:48
  36.9 3.6 %copy-start = (bf16[1,1,1,256,4,2,128]{6,5,4,3,2,1,0:T(2,128)(2,1)S(1)}, bf16[1,1,1,256,4,2,128]{6,5,4,3,2,1,0:T(2,128)(2,1)}, u32[]{:S(2)}) copy-start(bf16[1,1,1,256,4,2,128]{6,5,4,3,2,1,0:T(2,128)(2,1)} %param.5) | copy-start | bytes 1572868
  36.9 12.6 %all-to-all-start.4 = ((bf16[4,4,20,4,2,128]{5,4,3,2,1,0:T(2,128)(2,1)}), bf16[4,4,20,4,2,128]{5,4,3,2,1,0:T(2,128)(2,1)S(1)}, u32[]{:S(2)}, u32[]{:S(2)}) async-start(bf16[4,4,20,4,2,128]{5,4,3,2,1,0:T(2,128)(2,1)} %copy.58), calls=%async_computation.4 | async-start | bytes 1310720 | tf_op jit(solution)/shard_map/all_to_all | solution.py:42
  49.5 11.6 %all-to-all-start.2 = ((bf16[4,4,20,4,2,128]{5,4,3,2,1,0:T(2,128)(2,1)}), bf16[4,4,20,4,2,128]{5,4,3,2,1,0:T(2,128)(2,1)S(1)}, u32[]{:S(2)}, u32[]{:S(2)}) async-start(bf16[4,4,20,4,2,128]{5,4,3,2,1,0:T(2,128)(2,1)} %copy.52), calls=%async_computation.2 | async-start | bytes 1310720 | tf_op jit(solution)/shard_map/all_to_all | solution.py:35
  61.1 18.5 %all-to-all-start.5 = ((bf16[4,4,20,4,2,128]{5,4,3,2,0,1:T(2,128)(2,1)}), bf16[4,4,20,4,2,128]{5,4,3,2,0,1:T(2,128)(2,1)S(1)}, u32[]{:S(2)}, u32[]{:S(2)}) async-start(bf16[4,4,20,4,2,128]{5,4,3,2,0,1:T(2,128)(2,1)} %copy.59), calls=%async_computation.5 | async-start | bytes 1310720 | tf_op jit(solution)/shard_map/all_to_all | solution.py:41
  79.7 18.2 %all-to-all-start.3 = ((bf16[4,4,20,4,2,128]{5,4,3,2,0,1:T(2,128)(2,1)}), bf16[4,4,20,4,2,128]{5,4,3,2,0,1:T(2,128)(2,1)S(1)}, u32[]{:S(2)}, u32[]{:S(2)}) async-start(bf16[4,4,20,4,2,128]{5,4,3,2,0,1:T(2,128)(2,1)} %copy.53), calls=%async_computation.3 | async-start | bytes 1310720 | tf_op jit(solution)/shard_map/all_to_all | solution.py:34
  83.2 33.3 %all-reduce.7.cloned.1.call-start = ((), (), s32[]{:S(2)}) async-start(), calls=%async_computation.8 | async-start | bytes 131072 | tf_op jit(solution)/shard_map/psum | solution.py:139
  117.3 5.9 %collective-permute-start = (f32[4,1,128]{2,1,0:T(1,128)S(1)}, f32[4,1,128]{2,1,0:T(1,128)S(1)}, u32[]{:S(2)}, u32[]{:S(2)}) collective-permute-start(f32[4,1,128]{2,1,0:T(1,128)S(1)} %get-tuple-element.21), channel_id=1, source_target_pairs={{4,0},{8,4},{12,8},{5,1},{9,5},{13,9},{6,2},{10,6},{14,10},{7,3},{... | collective-permute-start | bytes 6152 | tf_op jit(solution)/shard_map/ppermute | solution.py:22
  118.6 5.8 %collective-permute-start.1 = (f32[4,1,128]{2,1,0:T(1,128)S(1)}, f32[4,1,128]{2,1,0:T(1,128)S(1)}, u32[]{:S(2)}, u32[]{:S(2)}) collective-permute-start(f32[4,1,128]{2,1,0:T(1,128)S(1)} %get-tuple-element.20), channel_id=1, source_target_pairs={{0,4},{4,8},{8,12},{1,5},{5,9},{9,13},{2,6},{6,10},{10,14},{3,7},{... | collective-permute-start | bytes 6152 | tf_op jit(solution)/shard_map/ppermute | solution.py:20
  124.5 6.0 %collective-permute-start.2 = (f32[4,18,1]{2,1,0:T(8,128)S(1)}, f32[4,18,1]{2,1,0:T(8,128)S(1)}, u32[]{:S(2)}, u32[]{:S(2)}) collective-permute-start(f32[4,18,1]{2,1,0:T(8,128)S(1)} %get-tuple-element.12), channel_id=1, source_target_pairs={{1,0},{2,1},{3,2},{5,4},{6,5},{7,6},{9,8},{10,9},{11,10},{13,12},{... | collective-permute-start | bytes 872 | tf_op jit(solution)/shard_map/ppermute | solution.py:22
  125.8 6.3 %collective-permute-start.3 = (f32[4,18,1]{2,1,0:T(8,128)S(1)}, f32[4,18,1]{2,1,0:T(8,128)S(1)}, u32[]{:S(2)}, u32[]{:S(2)}) collective-permute-start(f32[4,18,1]{2,1,0:T(8,128)S(1)} %get-tuple-element.13), channel_id=1, source_target_pairs={{0,1},{1,2},{2,3},{4,5},{5,6},{6,7},{8,9},{9,10},{10,11},{12,13},{... | collective-permute-start | bytes 872 | tf_op jit(solution)/shard_map/ppermute | solution.py:20
  132.2 48.7 %copy-start.1 = (f32[4,16,128]{2,1,0:T(8,128)S(1)}, f32[4,16,128]{2,1,0:T(8,128)}, u32[]{:S(2)}) copy-start(f32[4,16,128]{2,1,0:T(8,128)} %param.9) | copy-start | bytes 98308
  132.2 6.5 %collective-permute-start.4 = (f32[4,1,128]{2,1,0:T(1,128)S(1)}, f32[4,1,128]{2,1,0:T(1,128)S(1)}, u32[]{:S(2)}, u32[]{:S(2)}) collective-permute-start(f32[4,1,128]{2,1,0:T(1,128)S(1)} %get-tuple-element.19), channel_id=1, source_target_pairs={{4,0},{8,4},{12,8},{5,1},{9,5},{13,9},{6,2},{10,6},{14,10},{7,3},{... | collective-permute-start | bytes 6152 | tf_op jit(solution)/shard_map/ppermute | solution.py:22
  133.5 6.5 %collective-permute-start.5 = (f32[4,1,128]{2,1,0:T(1,128)S(1)}, f32[4,1,128]{2,1,0:T(1,128)S(1)}, u32[]{:S(2)}, u32[]{:S(2)}) collective-permute-start(f32[4,1,128]{2,1,0:T(1,128)S(1)} %get-tuple-element.18), channel_id=1, source_target_pairs={{0,4},{4,8},{8,12},{1,5},{5,9},{9,13},{2,6},{6,10},{10,14},{3,7},{... | collective-permute-start | bytes 6152 | tf_op jit(solution)/shard_map/ppermute | solution.py:20
  140.1 6.3 %collective-permute-start.6 = (f32[4,18,1]{2,1,0:T(8,128)S(1)}, f32[4,18,1]{2,1,0:T(8,128)S(1)}, u32[]{:S(2)}, u32[]{:S(2)}) collective-permute-start(f32[4,18,1]{2,1,0:T(8,128)S(1)} %get-tuple-element.10), channel_id=1, source_target_pairs={{1,0},{2,1},{3,2},{5,4},{6,5},{7,6},{9,8},{10,9},{11,10},{13,12},{... | collective-permute-start | bytes 872 | tf_op jit(solution)/shard_map/ppermute | solution.py:22
  141.4 6.6 %collective-permute-start.7 = (f32[4,18,1]{2,1,0:T(8,128)S(1)}, f32[4,18,1]{2,1,0:T(8,128)S(1)}, u32[]{:S(2)}, u32[]{:S(2)}) collective-permute-start(f32[4,18,1]{2,1,0:T(8,128)S(1)} %get-tuple-element.11), channel_id=1, source_target_pairs={{0,1},{1,2},{2,3},{4,5},{5,6},{6,7},{8,9},{9,10},{10,11},{12,13},{... | collective-permute-start | bytes 872 | tf_op jit(solution)/shard_map/ppermute | solution.py:20
  148.1 7.0 %collective-permute-start.8 = (f32[4,1,128]{2,1,0:T(1,128)S(1)}, f32[4,1,128]{2,1,0:T(1,128)S(1)}, u32[]{:S(2)}, u32[]{:S(2)}) collective-permute-start(f32[4,1,128]{2,1,0:T(1,128)S(1)} %get-tuple-element.17), channel_id=1, source_target_pairs={{4,0},{8,4},{12,8},{5,1},{9,5},{13,9},{6,2},{10,6},{14,10},{7,3},{... | collective-permute-start | bytes 6152 | tf_op jit(solution)/shard_map/ppermute | solution.py:22
  149.4 7.0 %collective-permute-start.9 = (f32[4,1,128]{2,1,0:T(1,128)S(1)}, f32[4,1,128]{2,1,0:T(1,128)S(1)}, u32[]{:S(2)}, u32[]{:S(2)}) collective-permute-start(f32[4,1,128]{2,1,0:T(1,128)S(1)} %get-tuple-element.16), channel_id=1, source_target_pairs={{0,4},{4,8},{8,12},{1,5},{5,9},{9,13},{2,6},{6,10},{10,14},{3,7},{... | collective-permute-start | bytes 6152 | tf_op jit(solution)/shard_map/ppermute | solution.py:20
  156.5 6.3 %collective-permute-start.10 = (f32[4,18,1]{2,1,0:T(8,128)S(1)}, f32[4,18,1]{2,1,0:T(8,128)S(1)}, u32[]{:S(2)}, u32[]{:S(2)}) collective-permute-start(f32[4,18,1]{2,1,0:T(8,128)S(1)} %get-tuple-element.8), channel_id=1, source_target_pairs={{1,0},{2,1},{3,2},{5,4},{6,5},{7,6},{9,8},{10,9},{11,10},{13,12},{... | collective-permute-start | bytes 872 | tf_op jit(solution)/shard_map/ppermute | solution.py:22
  157.8 6.6 %collective-permute-start.11 = (f32[4,18,1]{2,1,0:T(8,128)S(1)}, f32[4,18,1]{2,1,0:T(8,128)S(1)}, u32[]{:S(2)}, u32[]{:S(2)}) collective-permute-start(f32[4,18,1]{2,1,0:T(8,128)S(1)} %get-tuple-element.9), channel_id=1, source_target_pairs={{0,1},{1,2},{2,3},{4,5},{5,6},{6,7},{8,9},{9,10},{10,11},{12,13},{... | collective-permute-start | bytes 872 | tf_op jit(solution)/shard_map/ppermute | solution.py:20
  164.6 7.0 %collective-permute-start.12 = (f32[4,1,128]{2,1,0:T(1,128)S(1)}, f32[4,1,128]{2,1,0:T(1,128)S(1)}, u32[]{:S(2)}, u32[]{:S(2)}) collective-permute-start(f32[4,1,128]{2,1,0:T(1,128)S(1)} %get-tuple-element.15), channel_id=1, source_target_pairs={{4,0},{8,4},{12,8},{5,1},{9,5},{13,9},{6,2},{10,6},{14,10},{7,3},{... | collective-permute-start | bytes 6152 | tf_op jit(solution)/shard_map/ppermute | solution.py:22
  165.9 7.0 %collective-permute-start.13 = (f32[4,1,128]{2,1,0:T(1,128)S(1)}, f32[4,1,128]{2,1,0:T(1,128)S(1)}, u32[]{:S(2)}, u32[]{:S(2)}) collective-permute-start(f32[4,1,128]{2,1,0:T(1,128)S(1)} %get-tuple-element.14), channel_id=1, source_target_pairs={{0,4},{4,8},{8,12},{1,5},{5,9},{9,13},{2,6},{6,10},{10,14},{3,7},{... | collective-permute-start | bytes 6152 | tf_op jit(solution)/shard_map/ppermute | solution.py:20
  172.9 6.3 %collective-permute-start.14 = (f32[4,18,1]{2,1,0:T(8,128)S(1)}, f32[4,18,1]{2,1,0:T(8,128)S(1)}, u32[]{:S(2)}, u32[]{:S(2)}) collective-permute-start(f32[4,18,1]{2,1,0:T(8,128)S(1)} %get-tuple-element.6), channel_id=1, source_target_pairs={{1,0},{2,1},{3,2},{5,4},{6,5},{7,6},{9,8},{10,9},{11,10},{13,12},{... | collective-permute-start | bytes 872 | tf_op jit(solution)/shard_map/ppermute | solution.py:22
  174.2 6.6 %collective-permute-start.15 = (f32[4,18,1]{2,1,0:T(8,128)S(1)}, f32[4,18,1]{2,1,0:T(8,128)S(1)}, u32[]{:S(2)}, u32[]{:S(2)}) collective-permute-start(f32[4,18,1]{2,1,0:T(8,128)S(1)} %get-tuple-element.7), channel_id=1, source_target_pairs={{0,1},{1,2},{2,3},{4,5},{5,6},{6,7},{8,9},{9,10},{10,11},{12,13},{... | collective-permute-start | bytes 872 | tf_op jit(solution)/shard_map/ppermute | solution.py:20
  198.1 6.8 %copy-start.2 = (s32[1,1,1,256]{3,2,1,0:T(1,128)S(1)}, s32[1,1,1,256]{3,2,1,0:T(1,128)}, u32[]{:S(2)}) copy-start(s32[1,1,1,256]{3,2,1,0:T(1,128)} %param.7) | copy-start | bytes 3076
  198.1 18.5 %all-to-all-start.7 = ((bf16[4,4,20,4,2,128]{5,4,3,2,0,1:T(2,128)(2,1)}), bf16[4,4,20,4,2,128]{5,4,3,2,0,1:T(2,128)(2,1)S(1)}, u32[]{:S(2)}, u32[]{:S(2)}) async-start(bf16[4,4,20,4,2,128]{5,4,3,2,0,1:T(2,128)(2,1)} %copy.64), calls=%async_computation.7 | async-start | bytes 1310720 | tf_op jit(solution)/shard_map/all_to_all | solution.py:65
Sparse Core Ops, SparseCore 0:
  100.2 16.1 all-reduce.6
where the time goes:
time: 229 us; the launch traced here: 227 us
  starting transfers between devices  78.5 us (34%)
  waiting for transfers between devices  70.8 us (31%)
  local copies, waits for them, and re-layouts  32.6 us (14%)
  blocking collectives  24 us (10%)
  between operations  14.4 us (6%)
  other arithmetic  6.4 us (3%)
    ppermute x8, starting transfers between devices, with_halo(): lax.ppermute(tail, axis, [(i, (i + 1) % count) for i in range(ends)])  40.3 us
    psum x1, waiting for transfers between devices, local(): lax.psum((to_tile(grad_sum), to_tile(illum_sum)), 'group')  16.3 us
    all_to_all x1, blocking collectives, send_back(): lax.all_to_all(sectioned_back, 'gx', split_axis=0, concat_axis=0, tiled=T...  14.3 us
    all_to_all x1, waiting for transfers between devices, deliver(): lax.all_to_all(lax.all_to_all(sectioned_grad, 'gx', split_axis=0, concat_...  12.3 us
    all_to_all x1, waiting for transfers between devices, deliver(): lax.all_to_all(lax.all_to_all(sectioned_illum, 'gx', split_axis=0, concat...  12.3 us
    all_to_all x1, waiting for transfers between devices, send_back(): lax.all_to_all(lax.all_to_all(sectioned_back, 'gx', split_axis=0, concat_...  11.7 us
    ppermute x8, waiting for transfers between devices, with_halo(): lax.ppermute(tail, axis, [(i, (i + 1) % count) for i in range(ends)])  11.5 us
    ppermute x8, starting transfers between devices, with_halo(): lax.ppermute(head, axis, [((i + 1) % count, i) for i in range(ends)])  10.3 us
  transfers between devices with their start and end apart: 23, of which 17 were waited for; matrix products, arithmetic and copies ran while one was open for 11% of the time, Pallas kernels for 0%

commit v1 on v0

--- a/solution.py
+++ b/solution.py
@@ -7,6 +7,32 @@
 damping = 10.0
 smooth_rate = 0.12
 step_length = 24.0
+
+
+def launch_unit(frame_in, at_axis, point):
+    y = frame_in.shape
+    return jnp.moveaxis(
+        frame_in.reshape(*y[:at_axis], point, y[at_axis] // point, *y[at_axis + 1 :]), at_axis, 0
+    )
+
+
+def define_rows(inputs, axis_no):
+    item_now = list(inputs.shape[1:])
+    item_now[axis_no] *= inputs.shape[0]
+    return jnp.moveaxis(inputs, 0, axis_no).reshape(item_now)
+
+
+def field_choose(target, shard_axis, message, x_local):
+    current_block = jax.lax.axis_size(shard_axis)
+    h_now, oldest = (current_block, jax.lax.axis_index(shard_axis))
+    upper = launch_unit(target, message, h_now)
+    runs = [upper[oldest]]
+    for idx in range(1, h_now):
+        n_now = upper[oldest ^ idx]
+        value_now = jax.lax.ppermute(n_now, shard_axis, [(jj, jj ^ idx) for jj in range(h_now)])
+        runs.append(value_now)
+    upper = jnp.stack(runs, axis=0)[oldest ^ jnp.arange(h_now)]
+    return define_rows(upper, x_local)
 
 
 def with_halo(cells, sides, width):
@@ -45,12 +71,11 @@
             concat_axis=1,
             tiled=True,
         ),
-        lax.all_to_all(
+        field_choose(
             lax.all_to_all(sectioned_patch, "gx", split_axis=0, concat_axis=0, tiled=True),
             "gy",
-            split_axis=1,
-            concat_axis=1,
-            tiled=True,
+            1,
+            1,
         ),
     )
     return (

time: 229 us -> 227 us (level)
  blocking collectives: 24 us -> 14.3 us
  waiting for transfers between devices: 70.8 us -> 74.7 us
  starting transfers between devices: 78.5 us -> 82.3 us
    all_to_all x1, waiting for transfers between devices: 12.3 us -> 0.01 us  [deliver(): lax.all_to_all(lax.all_to_all(sectioned_grad, 'gx', split_axis=0, concat_...]
    ppermute x0 -> x3, waiting for transfers between devices: none -> 11.8 us  [field_choose(): jax.lax.ppermute(n_now, shard_axis, [(jj, jj ^ idx) for jj in range(h_now)])]
    all_to_all x1 -> x0, blocking collectives: 9.66 us -> none  [deliver(): lax.all_to_all(sectioned_patch, 'gx', split_axis=0, concat_axis=0, tiled=...]
    ppermute x0 -> x3, starting transfers between devices: none -> 4.45 us  [field_choose(): jax.lax.ppermute(n_now, shard_axis, [(jj, jj ^ idx) for jj in range(h_now)])]
    ppermute x8, waiting for transfers between devices: 0.52 us -> 4.64 us  [with_halo(): lax.ppermute(head, axis, [((i + 1) % count, i) for i in range(ends)])]
  transfers between devices with their start and end apart: 23 -> 26, of which waited for: 17 -> 18; matrix products, arithmetic and copies ran while one was open for 11% -> 11% of each run, Pallas kernels for 0% -> 0%
where the time goes in v1:
time: 227 us; the launch traced here: 226 us
  starting transfers between devices  82.3 us (36%)
  waiting for transfers between devices  74.7 us (33%)
  local copies, waits for them, and re-layouts  33.1 us (15%)
  between operations  14.4 us (6%)
  blocking collectives  14.3 us (6%)
  other arithmetic  6.41 us (3%)
    ppermute x8, starting transfers between devices, with_halo(): lax.ppermute(tail, axis, [(i, (i + 1) % count) for i in range(ends)])  39.3 us
    psum x1, waiting for transfers between devices, local(): lax.psum((to_tile(grad_sum), to_tile(illum_sum)), 'group')  15.1 us
    all_to_all x1, blocking collectives, send_back(): lax.all_to_all(sectioned_back, 'gx', split_axis=0, concat_axis=0, tiled=T...  14.3 us
    all_to_all x1, waiting for transfers between devices, deliver(): lax.all_to_all(lax.all_to_all(sectioned_illum, 'gx', split_axis=0, concat...  14.1 us
    ppermute x3, waiting for transfers between devices, field_choose(): jax.lax.ppermute(n_now, shard_axis, [(jj, jj ^ idx) for jj in range(h_now)])  11.8 us
    all_to_all x1, waiting for transfers between devices, send_back(): lax.all_to_all(lax.all_to_all(sectioned_back, 'gx', split_axis=0, concat_...  11.7 us
    ppermute x8, waiting for transfers between devices, with_halo(): lax.ppermute(tail, axis, [(i, (i + 1) % count) for i in range(ends)])  10.4 us
    ppermute x8, starting transfers between devices, with_halo(): lax.ppermute(head, axis, [((i + 1) % count, i) for i in range(ends)])  10.3 us
  transfers between devices with their start and end apart: 26, of which 18 were waited for; matrix products, arithmetic and copies ran while one was open for 11% of the time, Pallas kernels for 0%

profile of v1, /device:TPU:0, one launch (start us, length us, event | category | flops | bytes accessed | tf_op | source)
XLA Modules:
  0.0 226.1 jit_solution(12489800730515829734)
XLA Ops:
  7.2 0.7 fusion.38
  7.8 0.6 reduce-window.6
  8.6 0.8 fusion.37
  9.4 0.7 compare_select_fusion
  10.1 1.6 scatter_custom_fusion
  11.7 0.7 reshape.129
  12.4 5.2 %all-to-all-start = ((s32[4,4,20]{2,1,0:T(4,128)}), s32[4,4,20]{2,1,0:T(4,128)S(1)}, u32[]{:S(2)}, u32[]{:S(2)}) async-start(s32[4,4,20]{2,1,0:T(4,128)} %reshape.129), calls=%async_computation | async-start | bytes 16384 | tf_op jit(solution)/shard_map/all_to_all | solution.py:75
  17.5 1.2 copy.57
  18.9 7.1 %scatter_fusion.1 = bf16[320,4,2,128]{3,1,2,0:T(4,128)(2,1)S(1)} fusion(bf16[320,4,2,128]{3,1,2,0:T(4,128)(2,1)S(1)} %broadcast.138.clone.1, s32[256]{0:T(256)S(1)} %bitcast.83, bf16[256,4,2,128]{3,1,2,0:T(4,128)(2,1)S(1)} %copy.57), kind=kCustom, calls=%fused_computation.4 | custom fusion | bytes 1573888 | tf_op jit(solution)/shard_map/scatter | solution.py:141
  26.0 1.5 copy.58
  27.5 4.3 %all-to-all-start.3 = ((bf16[4,4,20,4,2,128]{5,4,3,2,1,0:T(2,128)(2,1)}), bf16[4,4,20,4,2,128]{5,4,3,2,1,0:T(2,128)(2,1)S(1)}, u32[]{:S(2)}, u32[]{:S(2)}) async-start(bf16[4,4,20,4,2,128]{5,4,3,2,1,0:T(2,128)(2,1)} %copy.58), calls=%async_computation.3 | async-start | bytes 1310720 | tf_op jit(solution)/shard_map/all_to_all | solution.py:68
  32.2 7.1 %scatter_fusion = bf16[320,4,2,128]{3,1,2,0:T(4,128)(2,1)S(1)} fusion(bf16[320,4,2,128]{3,1,2,0:T(4,128)(2,1)S(1)} %broadcast.138.clone, s32[256]{0:T(256)S(1)} %bitcast.84, bf16[256,4,2,128]{3,1,2,0:T(4,128)(2,1)S(1)} %copy.51), kind=kCustom, calls=%fused_computation.3 | custom fusion | bytes 1573888 | tf_op jit(solution)/shard_map/scatter | solution.py:136
  39.3 1.5 copy.52
  40.8 4.2 %all-to-all-start.1 = ((bf16[4,4,20,4,2,128]{5,4,3,2,1,0:T(2,128)(2,1)}), bf16[4,4,20,4,2,128]{5,4,3,2,1,0:T(2,128)(2,1)S(1)}, u32[]{:S(2)}, u32[]{:S(2)}) async-start(bf16[4,4,20,4,2,128]{5,4,3,2,1,0:T(2,128)(2,1)} %copy.52), calls=%async_computation.1 | async-start | bytes 1310720 | tf_op jit(solution)/shard_map/all_to_all | solution.py:61
  45.0 1.3 copy.59
  46.4 7.0 %all-to-all-done.1 = bf16[4,4,20,4,2,128]{5,4,3,2,1,0:T(2,128)(2,1)S(1)} async-done(((bf16[4,4,20,4,2,128]{5,4,3,2,1,0:T(2,128)(2,1)}), bf16[4,4,20,4,2,128]{5,4,3,2,1,0:T(2,128)(2,1)S(1)}, u32[]{:S(2)}, u32[]{:S(2)}) %all-to-all-start.1) | async-done | bytes 655392 | tf_op jit(solution)/shard_map/all_to_all | solution.py:61
  53.3 4.9 %all-to-all-start.4 = ((bf16[4,4,20,4,2,128]{5,4,3,2,0,1:T(2,128)(2,1)}), bf16[4,4,20,4,2,128]{5,4,3,2,0,1:T(2,128)(2,1)S(1)}, u32[]{:S(2)}, u32[]{:S(2)}) async-start(bf16[4,4,20,4,2,128]{5,4,3,2,0,1:T(2,128)(2,1)} %copy.59), calls=%async_computation.4 | async-start | bytes 1310720 | tf_op jit(solution)/shard_map/all_to_all | solution.py:67
  58.2 1.3 copy.53
  59.5 14.1 %all-to-all-done.4 = bf16[4,4,20,4,2,128]{5,4,3,2,0,1:T(2,128)(2,1)S(1)} async-done(((bf16[4,4,20,4,2,128]{5,4,3,2,0,1:T(2,128)(2,1)}), bf16[4,4,20,4,2,128]{5,4,3,2,0,1:T(2,128)(2,1)S(1)}, u32[]{:S(2)}, u32[]{:S(2)}) %all-to-all-start.4) | async-done | bytes 655392 | tf_op jit(solution)/shard_map/all_to_all | solution.py:67
  73.6 3.5 %all-to-all-start.2 = ((bf16[4,4,20,4,2,128]{5,4,3,2,0,1:T(2,128)(2,1)}), bf16[4,4,20,4,2,128]{5,4,3,2,0,1:T(2,128)(2,1)S(1)}, u32[]{:S(2)}, u32[]{:S(2)}) async-start(bf16[4,4,20,4,2,128]{5,4,3,2,0,1:T(2,128)(2,1)} %copy.53), calls=%async_computation.2 | async-start | bytes 1310720 | tf_op jit(solution)/shard_map/all_to_all | solution.py:60
  77.2 3.8 %collective-permute-start.2 = (s32[4,1,20]{2,1,0:T(1,128)S(1)}, s32[4,1,20]{2,1,0:T(1,128)S(1)}, u32[]{:S(2)}, u32[]{:S(2)}) collective-permute-start(s32[4,1,20]{2,1,0:T(1,128)S(1)} %get-tuple-element.23), channel_id=1, source_target_pairs={{0,3},{1,2},{2,1},{3,0},{4,7},{5,6},{6,5},{7,4},{8,11},{9,10},{10,... | collective-permute-start | bytes 968 | tf_op jit(solution)/shard_map/ppermute | solution.py:32
  81.0 0.7 collective-permute-start.1
  81.7 9.3 %collective-permute-done.2 = s32[4,1,20]{2,1,0:T(1,128)S(1)} collective-permute-done((s32[4,1,20]{2,1,0:T(1,128)S(1)}, s32[4,1,20]{2,1,0:T(1,128)S(1)}, u32[]{:S(2)}, u32[]{:S(2)}) %collective-permute-start.2) | collective-permute-done | bytes 352 | tf_op jit(solution)/shard_map/ppermute | solution.py:32
  91.0 2.5 %collective-permute-done.1 = s32[4,1,20]{2,1,0:T(1,128)S(1)} collective-permute-done((s32[4,1,20]{2,1,0:T(1,128)S(1)}, s32[4,1,20]{2,1,0:T(1,128)S(1)}, u32[]{:S(2)}, u32[]{:S(2)}) %collective-permute-start.1) | collective-permute-done | bytes 352 | tf_op jit(solution)/shard_map/ppermute | solution.py:32
  93.5 0.6 gather_fusion
  94.2 0.5 copy.60
  94.6 0.5 reshape_reshape.10
  95.1 0.5 dot_general.21
  95.8 0.6 copy.62
  96.4 0.5 copy.54
  98.0 0.6 copy.56
  98.7 15.1 %all-reduce.7.cloned.1.call-done = (f32[4,16,128]{2,1,0:T(8,128)}, f32[4,16,128]{2,1,0:T(8,128)}) async-done(((f32[4,16,128]{2,1,0:T(8,128)}, f32[4,16,128]{2,1,0:T(8,128)}), (f32[4,16,128]{2,1,0:T(8,128)}, f32[4,16,128]{2,1,0:T(8,128)})) %all-reduce.7.cloned.1.call-update) | async-done | bytes 65552 | tf_op jit(solution)/shard_map/psum | solution.py:164
  113.8 0.8 add_divide_fusion
  114.6 1.3 collective-permute-start.3
  115.9 4.5 %collective-permute-start.4 = (f32[4,1,128]{2,1,0:T(1,128)S(1)}, f32[4,1,128]{2,1,0:T(1,128)S(1)}, u32[]{:S(2)}, u32[]{:S(2)}) collective-permute-start(f32[4,1,128]{2,1,0:T(1,128)S(1)} %get-tuple-element.20), channel_id=1, source_target_pairs={{0,4},{4,8},{8,12},{1,5},{5,9},{9,13},{2,6},{6,10},{10,14},{3,7},{... | collective-permute-start | bytes 6152 | tf_op jit(solution)/shard_map/ppermute | solution.py:46
  120.5 1.3 collective-permute-done.4
  121.9 1.3 collective-permute-start.5
  123.2 4.5 %collective-permute-start.6 = (f32[4,18,1]{2,1,0:T(8,128)S(1)}, f32[4,18,1]{2,1,0:T(8,128)S(1)}, u32[]{:S(2)}, u32[]{:S(2)}) collective-permute-start(f32[4,18,1]{2,1,0:T(8,128)S(1)} %get-tuple-element.13), channel_id=1, source_target_pairs={{0,1},{1,2},{2,3},{4,5},{5,6},{6,7},{8,9},{9,10},{10,11},{12,13},{... | collective-permute-start | bytes 872 | tf_op jit(solution)/shard_map/ppermute | solution.py:46
  127.8 1.6 collective-permute-done.6
  129.6 1.3 collective-permute-start.7
  130.9 5.2 %collective-permute-start.8 = (f32[4,1,128]{2,1,0:T(1,128)S(1)}, f32[4,1,128]{2,1,0:T(1,128)S(1)}, u32[]{:S(2)}, u32[]{:S(2)}) collective-permute-start(f32[4,1,128]{2,1,0:T(1,128)S(1)} %get-tuple-element.18), channel_id=1, source_target_pairs={{0,4},{4,8},{8,12},{1,5},{5,9},{9,13},{2,6},{6,10},{10,14},{3,7},{... | collective-permute-start | bytes 6152 | tf_op jit(solution)/shard_map/ppermute | solution.py:46
  136.1 1.3 collective-permute-done.8
  137.4 4.2 %collective-permute-start.10 = (f32[4,18,1]{2,1,0:T(8,128)S(1)}, f32[4,18,1]{2,1,0:T(8,128)S(1)}, u32[]{:S(2)}, u32[]{:S(2)}) collective-permute-start(f32[4,18,1]{2,1,0:T(8,128)S(1)} %get-tuple-element.11), channel_id=1, source_target_pairs={{0,1},{1,2},{2,3},{4,5},{5,6},{6,7},{8,9},{9,10},{10,11},{12,13},{... | collective-permute-start | bytes 872 | tf_op jit(solution)/shard_map/ppermute | solution.py:46
  141.7 1.3 collective-permute-start.9
  143.4 4.3 %collective-permute-done.9 = f32[4,18,1]{2,1,0:T(8,128)S(1)} collective-permute-done((f32[4,18,1]{2,1,0:T(8,128)S(1)}, f32[4,18,1]{2,1,0:T(8,128)S(1)}, u32[]{:S(2)}, u32[]{:S(2)}) %collective-permute-start.9) | collective-permute-done | bytes 320 | tf_op jit(solution)/shard_map/ppermute | solution.py:48
  147.8 1.3 collective-permute-start.11
  149.1 5.7 %collective-permute-start.12 = (f32[4,1,128]{2,1,0:T(1,128)S(1)}, f32[4,1,128]{2,1,0:T(1,128)S(1)}, u32[]{:S(2)}, u32[]{:S(2)}) collective-permute-start(f32[4,1,128]{2,1,0:T(1,128)S(1)} %get-tuple-element.16), channel_id=1, source_target_pairs={{0,4},{4,8},{8,12},{1,5},{5,9},{9,13},{2,6},{6,10},{10,14},{3,7},{... | collective-permute-start | bytes 6152 | tf_op jit(solution)/shard_map/ppermute | solution.py:46
  154.8 1.3 collective-permute-done.12
  156.2 1.3 collective-permute-start.13
  157.5 4.5 %collective-permute-start.14 = (f32[4,18,1]{2,1,0:T(8,128)S(1)}, f32[4,18,1]{2,1,0:T(8,128)S(1)}, u32[]{:S(2)}, u32[]{:S(2)}) collective-permute-start(f32[4,18,1]{2,1,0:T(8,128)S(1)} %get-tuple-element.9), channel_id=1, source_target_pairs={{0,1},{1,2},{2,3},{4,5},{5,6},{6,7},{8,9},{9,10},{10,11},{12,13},{... | collective-permute-start | bytes 872 | tf_op jit(solution)/shard_map/ppermute | solution.py:46
  162.2 1.6 collective-permute-done.14
  163.9 1.3 collective-permute-start.15
  165.2 5.7 %collective-permute-start.16 = (f32[4,1,128]{2,1,0:T(1,128)S(1)}, f32[4,1,128]{2,1,0:T(1,128)S(1)}, u32[]{:S(2)}, u32[]{:S(2)}) collective-permute-start(f32[4,1,128]{2,1,0:T(1,128)S(1)} %get-tuple-element.14), channel_id=1, source_target_pairs={{0,4},{4,8},{8,12},{1,5},{5,9},{9,13},{2,6},{6,10},{10,14},{3,7},{... | collective-permute-start | bytes 6152 | tf_op jit(solution)/shard_map/ppermute | solution.py:46
  170.9 1.3 collective-permute-done.16
  172.3 1.3 collective-permute-start.17
  173.6 4.9 %collective-permute-start.18 = (f32[4,18,1]{2,1,0:T(8,128)S(1)}, f32[4,18,1]{2,1,0:T(8,128)S(1)}, u32[]{:S(2)}, u32[]{:S(2)}) collective-permute-start(f32[4,18,1]{2,1,0:T(8,128)S(1)} %get-tuple-element.7), channel_id=1, source_target_pairs={{0,1},{1,2},{2,3},{4,5},{5,6},{6,7},{8,9},{9,10},{10,11},{12,13},{... | collective-permute-start | bytes 872 | tf_op jit(solution)/shard_map/ppermute | solution.py:46
  178.6 1.6 collective-permute-done.18
  180.2 0.7 fusion.48
  181.8 14.3 %all_to_all.35 = bf16[4,4,20,4,2,128]{5,4,3,2,1,0:T(2,128)(2,1)S(1)} all-to-all(bf16[4,4,20,4,2,128]{5,4,3,2,1,0:T(2,128)(2,1)S(1)} %reshape_reshape.11), channel_id=1, replica_groups=mesh['group'=2,'gx'=4,'gy'=4] {'gx'}, dimensions={0} | all-to-all | bytes 1310720 | tf_op jit(solution)/shard_map/all_to_all | solution.py:91
  196.1 1.3 copy.64
  197.5 6.1 %all-to-all-start.6 = ((bf16[4,4,20,4,2,128]{5,4,3,2,0,1:T(2,128)(2,1)}), bf16[4,4,20,4,2,128]{5,4,3,2,0,1:T(2,128)(2,1)S(1)}, u32[]{:S(2)}, u32[]{:S(2)}) async-start(bf16[4,4,20,4,2,128]{5,4,3,2,0,1:T(2,128)(2,1)} %copy.64), calls=%async_computation.6 | async-start | bytes 1310720 | tf_op jit(solution)/shard_map/all_to_all | solution.py:90
  203.6 11.7 %all-to-all-done.6 = bf16[4,4,20,4,2,128]{5,4,3,2,0,1:T(2,128)(2,1)S(1)} async-done(((bf16[4,4,20,4,2,128]{5,4,3,2,0,1:T(2,128)(2,1)}), bf16[4,4,20,4,2,128]{5,4,3,2,0,1:T(2,128)(2,1)S(1)}, u32[]{:S(2)}, u32[]{:S(2)}) %all-to-all-start.6) | async-done | bytes 655392 | tf_op jit(solution)/shard_map/all_to_all | solution.py:90
  215.7 1.7 gather_fusion.1
  217.5 1.7 broadcast_select_fusion
  (59 shorter events, 5.1 us)
Async XLA Ops:
  12.4 15.2 %all-to-all-start = ((s32[4,4,20]{2,1,0:T(4,128)}), s32[4,4,20]{2,1,0:T(4,128)S(1)}, u32[]{:S(2)}, u32[]{:S(2)}) async-start(s32[4,4,20]{2,1,0:T(4,128)} %reshape.129), calls=%async_computation | async-start | bytes 16384 | tf_op jit(solution)/shard_map/all_to_all | solution.py:75
  27.5 4.3 %copy-start = (bf16[1,1,1,256,4,2,128]{6,5,4,3,2,1,0:T(2,128)(2,1)S(1)}, bf16[1,1,1,256,4,2,128]{6,5,4,3,2,1,0:T(2,128)(2,1)}, u32[]{:S(2)}) copy-start(bf16[1,1,1,256,4,2,128]{6,5,4,3,2,1,0:T(2,128)(2,1)} %param.5) | copy-start | bytes 1572868
  27.5 13.3 %all-to-all-start.3 = ((bf16[4,4,20,4,2,128]{5,4,3,2,1,0:T(2,128)(2,1)}), bf16[4,4,20,4,2,128]{5,4,3,2,1,0:T(2,128)(2,1)S(1)}, u32[]{:S(2)}, u32[]{:S(2)}) async-start(bf16[4,4,20,4,2,128]{5,4,3,2,1,0:T(2,128)(2,1)} %copy.58), calls=%async_computation.3 | async-start | bytes 1310720 | tf_op jit(solution)/shard_map/all_to_all | solution.py:68
  40.8 12.5 %all-to-all-start.1 = ((bf16[4,4,20,4,2,128]{5,4,3,2,1,0:T(2,128)(2,1)}), bf16[4,4,20,4,2,128]{5,4,3,2,1,0:T(2,128)(2,1)S(1)}, u32[]{:S(2)}, u32[]{:S(2)}) async-start(bf16[4,4,20,4,2,128]{5,4,3,2,1,0:T(2,128)(2,1)} %copy.52), calls=%async_computation.1 | async-start | bytes 1310720 | tf_op jit(solution)/shard_map/all_to_all | solution.py:61
  53.3 20.3 %all-to-all-start.4 = ((bf16[4,4,20,4,2,128]{5,4,3,2,0,1:T(2,128)(2,1)}), bf16[4,4,20,4,2,128]{5,4,3,2,0,1:T(2,128)(2,1)S(1)}, u32[]{:S(2)}, u32[]{:S(2)}) async-start(bf16[4,4,20,4,2,128]{5,4,3,2,0,1:T(2,128)(2,1)} %copy.59), calls=%async_computation.4 | async-start | bytes 1310720 | tf_op jit(solution)/shard_map/all_to_all | solution.py:67
  73.6 22.8 %all-to-all-start.2 = ((bf16[4,4,20,4,2,128]{5,4,3,2,0,1:T(2,128)(2,1)}), bf16[4,4,20,4,2,128]{5,4,3,2,0,1:T(2,128)(2,1)S(1)}, u32[]{:S(2)}, u32[]{:S(2)}) async-start(bf16[4,4,20,4,2,128]{5,4,3,2,0,1:T(2,128)(2,1)} %copy.53), calls=%async_computation.2 | async-start | bytes 1310720 | tf_op jit(solution)/shard_map/all_to_all | solution.py:60
  77.1 36.7 %all-reduce.7.cloned.1.call-start = ((), (), s32[]{:S(2)}) async-start(), calls=%async_computation.7 | async-start | bytes 131072 | tf_op jit(solution)/shard_map/psum | solution.py:164
  77.2 13.8 %collective-permute-start.2 = (s32[4,1,20]{2,1,0:T(1,128)S(1)}, s32[4,1,20]{2,1,0:T(1,128)S(1)}, u32[]{:S(2)}, u32[]{:S(2)}) collective-permute-start(s32[4,1,20]{2,1,0:T(1,128)S(1)} %get-tuple-element.23), channel_id=1, source_target_pairs={{0,3},{1,2},{2,1},{3,0},{4,7},{5,6},{6,5},{7,4},{8,11},{9,10},{10,... | collective-permute-start | bytes 968 | tf_op jit(solution)/shard_map/ppermute | solution.py:32
  81.0 10.0 %collective-permute-start = (s32[4,1,20]{2,1,0:T(1,128)S(1)}, s32[4,1,20]{2,1,0:T(1,128)S(1)}, u32[]{:S(2)}, u32[]{:S(2)}) collective-permute-start(s32[4,1,20]{2,1,0:T(1,128)S(1)} %get-tuple-element.25), channel_id=1, source_target_pairs={{0,1},{1,0},{2,3},{3,2},{4,5},{5,4},{6,7},{7,6},{8,9},{9,8},{10,11... | collective-permute-start | bytes 968 | tf_op jit(solution)/shard_map/ppermute | solution.py:32
  81.0 12.5 %collective-permute-start.1 = (s32[4,1,20]{2,1,0:T(1,128)S(1)}, s32[4,1,20]{2,1,0:T(1,128)S(1)}, u32[]{:S(2)}, u32[]{:S(2)}) collective-permute-start(s32[4,1,20]{2,1,0:T(1,128)S(1)} %get-tuple-element.24), channel_id=1, source_target_pairs={{0,2},{1,3},{2,0},{3,1},{4,6},{5,7},{6,4},{7,5},{8,10},{9,11},{10,... | collective-permute-start | bytes 968 | tf_op jit(solution)/shard_map/ppermute | solution.py:32
  114.6 5.9 %collective-permute-start.3 = (f32[4,1,128]{2,1,0:T(1,128)S(1)}, f32[4,1,128]{2,1,0:T(1,128)S(1)}, u32[]{:S(2)}, u32[]{:S(2)}) collective-permute-start(f32[4,1,128]{2,1,0:T(1,128)S(1)} %get-tuple-element.21), channel_id=1, source_target_pairs={{4,0},{8,4},{12,8},{5,1},{9,5},{13,9},{6,2},{10,6},{14,10},{7,3},{... | collective-permute-start | bytes 6152 | tf_op jit(solution)/shard_map/ppermute | solution.py:48
  115.9 5.8 %collective-permute-start.4 = (f32[4,1,128]{2,1,0:T(1,128)S(1)}, f32[4,1,128]{2,1,0:T(1,128)S(1)}, u32[]{:S(2)}, u32[]{:S(2)}) collective-permute-start(f32[4,1,128]{2,1,0:T(1,128)S(1)} %get-tuple-element.20), channel_id=1, source_target_pairs={{0,4},{4,8},{8,12},{1,5},{5,9},{9,13},{2,6},{6,10},{10,14},{3,7},{... | collective-permute-start | bytes 6152 | tf_op jit(solution)/shard_map/ppermute | solution.py:46
  121.9 6.0 %collective-permute-start.5 = (f32[4,18,1]{2,1,0:T(8,128)S(1)}, f32[4,18,1]{2,1,0:T(8,128)S(1)}, u32[]{:S(2)}, u32[]{:S(2)}) collective-permute-start(f32[4,18,1]{2,1,0:T(8,128)S(1)} %get-tuple-element.12), channel_id=1, source_target_pairs={{1,0},{2,1},{3,2},{5,4},{6,5},{7,6},{9,8},{10,9},{11,10},{13,12},{... | collective-permute-start | bytes 872 | tf_op jit(solution)/shard_map/ppermute | solution.py:48
  123.2 6.3 %collective-permute-start.6 = (f32[4,18,1]{2,1,0:T(8,128)S(1)}, f32[4,18,1]{2,1,0:T(8,128)S(1)}, u32[]{:S(2)}, u32[]{:S(2)}) collective-permute-start(f32[4,18,1]{2,1,0:T(8,128)S(1)} %get-tuple-element.13), channel_id=1, source_target_pairs={{0,1},{1,2},{2,3},{4,5},{5,6},{6,7},{8,9},{9,10},{10,11},{12,13},{... | collective-permute-start | bytes 872 | tf_op jit(solution)/shard_map/ppermute | solution.py:46
  129.6 50.7 %copy-start.1 = (f32[4,16,128]{2,1,0:T(8,128)S(1)}, f32[4,16,128]{2,1,0:T(8,128)}, u32[]{:S(2)}) copy-start(f32[4,16,128]{2,1,0:T(8,128)} %param.9) | copy-start | bytes 98308
  129.6 6.5 %collective-permute-start.7 = (f32[4,1,128]{2,1,0:T(1,128)S(1)}, f32[4,1,128]{2,1,0:T(1,128)S(1)}, u32[]{:S(2)}, u32[]{:S(2)}) collective-permute-start(f32[4,1,128]{2,1,0:T(1,128)S(1)} %get-tuple-element.19), channel_id=1, source_target_pairs={{4,0},{8,4},{12,8},{5,1},{9,5},{13,9},{6,2},{10,6},{14,10},{7,3},{... | collective-permute-start | bytes 6152 | tf_op jit(solution)/shard_map/ppermute | solution.py:48
  130.9 6.5 %collective-permute-start.8 = (f32[4,1,128]{2,1,0:T(1,128)S(1)}, f32[4,1,128]{2,1,0:T(1,128)S(1)}, u32[]{:S(2)}, u32[]{:S(2)}) collective-permute-start(f32[4,1,128]{2,1,0:T(1,128)S(1)} %get-tuple-element.18), channel_id=1, source_target_pairs={{0,4},{4,8},{8,12},{1,5},{5,9},{9,13},{2,6},{6,10},{10,14},{3,7},{... | collective-permute-start | bytes 6152 | tf_op jit(solution)/shard_map/ppermute | solution.py:46
  137.4 6.0 %collective-permute-start.10 = (f32[4,18,1]{2,1,0:T(8,128)S(1)}, f32[4,18,1]{2,1,0:T(8,128)S(1)}, u32[]{:S(2)}, u32[]{:S(2)}) collective-permute-start(f32[4,18,1]{2,1,0:T(8,128)S(1)} %get-tuple-element.11), channel_id=1, source_target_pairs={{0,1},{1,2},{2,3},{4,5},{5,6},{6,7},{8,9},{9,10},{10,11},{12,13},{... | collective-permute-start | bytes 872 | tf_op jit(solution)/shard_map/ppermute | solution.py:46
  141.7 6.0 %collective-permute-start.9 = (f32[4,18,1]{2,1,0:T(8,128)S(1)}, f32[4,18,1]{2,1,0:T(8,128)S(1)}, u32[]{:S(2)}, u32[]{:S(2)}) collective-permute-start(f32[4,18,1]{2,1,0:T(8,128)S(1)} %get-tuple-element.10), channel_id=1, source_target_pairs={{1,0},{2,1},{3,2},{5,4},{6,5},{7,6},{9,8},{10,9},{11,10},{13,12},{... | collective-permute-start | bytes 872 | tf_op jit(solution)/shard_map/ppermute | solution.py:48
  147.8 7.0 %collective-permute-start.11 = (f32[4,1,128]{2,1,0:T(1,128)S(1)}, f32[4,1,128]{2,1,0:T(1,128)S(1)}, u32[]{:S(2)}, u32[]{:S(2)}) collective-permute-start(f32[4,1,128]{2,1,0:T(1,128)S(1)} %get-tuple-element.17), channel_id=1, source_target_pairs={{4,0},{8,4},{12,8},{5,1},{9,5},{13,9},{6,2},{10,6},{14,10},{7,3},{... | collective-permute-start | bytes 6152 | tf_op jit(solution)/shard_map/ppermute | solution.py:48
  149.1 7.0 %collective-permute-start.12 = (f32[4,1,128]{2,1,0:T(1,128)S(1)}, f32[4,1,128]{2,1,0:T(1,128)S(1)}, u32[]{:S(2)}, u32[]{:S(2)}) collective-permute-start(f32[4,1,128]{2,1,0:T(1,128)S(1)} %get-tuple-element.16), channel_id=1, source_target_pairs={{0,4},{4,8},{8,12},{1,5},{5,9},{9,13},{2,6},{6,10},{10,14},{3,7},{... | collective-permute-start | bytes 6152 | tf_op jit(solution)/shard_map/ppermute | solution.py:46
  156.2 6.0 %collective-permute-start.13 = (f32[4,18,1]{2,1,0:T(8,128)S(1)}, f32[4,18,1]{2,1,0:T(8,128)S(1)}, u32[]{:S(2)}, u32[]{:S(2)}) collective-permute-start(f32[4,18,1]{2,1,0:T(8,128)S(1)} %get-tuple-element.8), channel_id=1, source_target_pairs={{1,0},{2,1},{3,2},{5,4},{6,5},{7,6},{9,8},{10,9},{11,10},{13,12},{... | collective-permute-start | bytes 872 | tf_op jit(solution)/shard_map/ppermute | solution.py:48
  157.5 6.3 %collective-permute-start.14 = (f32[4,18,1]{2,1,0:T(8,128)S(1)}, f32[4,18,1]{2,1,0:T(8,128)S(1)}, u32[]{:S(2)}, u32[]{:S(2)}) collective-permute-start(f32[4,18,1]{2,1,0:T(8,128)S(1)} %get-tuple-element.9), channel_id=1, source_target_pairs={{0,1},{1,2},{2,3},{4,5},{5,6},{6,7},{8,9},{9,10},{10,11},{12,13},{... | collective-permute-start | bytes 872 | tf_op jit(solution)/shard_map/ppermute | solution.py:46
  163.9 7.0 %collective-permute-start.15 = (f32[4,1,128]{2,1,0:T(1,128)S(1)}, f32[4,1,128]{2,1,0:T(1,128)S(1)}, u32[]{:S(2)}, u32[]{:S(2)}) collective-permute-start(f32[4,1,128]{2,1,0:T(1,128)S(1)} %get-tuple-element.15), channel_id=1, source_target_pairs={{4,0},{8,4},{12,8},{5,1},{9,5},{13,9},{6,2},{10,6},{14,10},{7,3},{... | collective-permute-start | bytes 6152 | tf_op jit(solution)/shard_map/ppermute | solution.py:48
  165.2 7.0 %collective-permute-start.16 = (f32[4,1,128]{2,1,0:T(1,128)S(1)}, f32[4,1,128]{2,1,0:T(1,128)S(1)}, u32[]{:S(2)}, u32[]{:S(2)}) collective-permute-start(f32[4,1,128]{2,1,0:T(1,128)S(1)} %get-tuple-element.14), channel_id=1, source_target_pairs={{0,4},{4,8},{8,12},{1,5},{5,9},{9,13},{2,6},{6,10},{10,14},{3,7},{... | collective-permute-start | bytes 6152 | tf_op jit(solution)/shard_map/ppermute | solution.py:46
  172.3 6.3 %collective-permute-start.17 = (f32[4,18,1]{2,1,0:T(8,128)S(1)}, f32[4,18,1]{2,1,0:T(8,128)S(1)}, u32[]{:S(2)}, u32[]{:S(2)}) collective-permute-start(f32[4,18,1]{2,1,0:T(8,128)S(1)} %get-tuple-element.6), channel_id=1, source_target_pairs={{1,0},{2,1},{3,2},{5,4},{6,5},{7,6},{9,8},{10,9},{11,10},{13,12},{... | collective-permute-start | bytes 872 | tf_op jit(solution)/shard_map/ppermute | solution.py:48
  173.6 6.6 %collective-permute-start.18 = (f32[4,18,1]{2,1,0:T(8,128)S(1)}, f32[4,18,1]{2,1,0:T(8,128)S(1)}, u32[]{:S(2)}, u32[]{:S(2)}) collective-permute-start(f32[4,18,1]{2,1,0:T(8,128)S(1)} %get-tuple-element.7), channel_id=1, source_target_pairs={{0,1},{1,2},{2,3},{4,5},{5,6},{6,7},{8,9},{9,10},{10,11},{12,13},{... | collective-permute-start | bytes 872 | tf_op jit(solution)/shard_map/ppermute | solution.py:46
  197.5 6.1 %copy-start.2 = (s32[1,1,1,256]{3,2,1,0:T(1,128)S(1)}, s32[1,1,1,256]{3,2,1,0:T(1,128)}, u32[]{:S(2)}) copy-start(s32[1,1,1,256]{3,2,1,0:T(1,128)} %param.7) | copy-start | bytes 3076
  197.5 17.8 %all-to-all-start.6 = ((bf16[4,4,20,4,2,128]{5,4,3,2,0,1:T(2,128)(2,1)}), bf16[4,4,20,4,2,128]{5,4,3,2,0,1:T(2,128)(2,1)S(1)}, u32[]{:S(2)}, u32[]{:S(2)}) async-start(bf16[4,4,20,4,2,128]{5,4,3,2,0,1:T(2,128)(2,1)} %copy.64), calls=%async_computation.6 | async-start | bytes 1310720 | tf_op jit(solution)/shard_map/all_to_all | solution.py:90
Sparse Core Ops, SparseCore 0:
  98.8 14.9 all-reduce.6
